TPU v7x, 32 devices: a whole 2x2x4 slice. The times are simulated.
32 devices in a mesh: dp: 4 (over x, core), tensor: 8 (over z, y).
Axes of the slice: x: 2, y: 2, z: 4, core: 2. Of those that a mesh axis runs over, the one named last changes fastest.
Arguments:
- grad: bfloat16 [4, 576, 6144], P('dp', 'tensor'), as said below
- momentum: float32 [4, 576, 6144], P('dp', 'tensor'), may hold values from -6 to 6
- owner: int32 [4], replicated, may hold values from 0 to 3, each once
Outputs:
- update: bfloat16 [4, 576, 6144], P(None, 'tensor')
- new_momentum: float32 [4, 576, 6144], P('dp', 'tensor')
Inputs may be any that keep to these rules, and one draw needn't show every extreme that they name: owner names each matrix 0 to 3 exactly once. `grad`: gradient entries are finite; every matrix has full rank.
All inputs are finite; a program needn't handle non-finite values.
Results may differ from a plain program's by a relative error of at most 0.0013.
The roundings to bfloat16 on the way count: a program that leaves them out, or rounds other values in their place, can miss the bound.
Values may be sent and summed in bfloat16 or wider, within the bound.
No kernel may reach another device: no remote copies, remote signals or barrier semaphores. Data moves between devices by JAX's collectives and lax.ppermute only.
A program may use at most 64 MiB of HBM per device.

v0:
```python
import math
import jax
import jax.numpy as jnp
from jax import lax
from jax.sharding import PartitionSpec as P

M = 576
N = 6144
ITERS = 2
coef_a = 3.4445
coef_b = -4.775
coef_c = 2.0315
decay = 0.95
eps = 1e-07


def per_device(grad, momentum, owner):
    new_momentum = decay * momentum + grad.astype(jnp.float32)
    direction = grad.astype(jnp.float32) + decay * new_momentum
    total = lax.psum(jnp.sum(direction * direction), "tensor")
    rows_here = (direction[0] / (jnp.sqrt(total) + eps)).astype(jnp.bfloat16)
    columns = lax.all_to_all(rows_here, "tensor", split_axis=1, concat_axis=0, tiled=True)
    for step in range(ITERS):
        gram = lax.psum(
            jnp.dot(columns, columns.T, preferred_element_type=jnp.float32), "tensor"
        ).astype(jnp.bfloat16)
        square = jnp.dot(gram, gram, preferred_element_type=jnp.float32)
        poly = (coef_b * gram.astype(jnp.float32) + coef_c * square).astype(jnp.bfloat16)
        applied = jnp.dot(poly, columns, preferred_element_type=jnp.float32)
        columns = (coef_a * columns.astype(jnp.float32) + applied).astype(jnp.bfloat16)
    factor = 0.2 * math.sqrt(max(M, N))
    back_rows = lax.all_to_all(columns, "tensor", split_axis=0, concat_axis=1, tiled=True)
    scaled = (factor * back_rows.astype(jnp.float32)).astype(jnp.bfloat16)
    every_slot = lax.all_gather(scaled[None], "dp", axis=0, tiled=True)
    matrix_ids = jnp.arange(every_slot.shape[0], dtype=jnp.int32)
    selector = (owner[None, :] == matrix_ids[:, None]).astype(jnp.bfloat16)
    update = jnp.einsum(
        "mg,grn->mrn", selector, every_slot, preferred_element_type=jnp.float32
    ).astype(jnp.bfloat16)
    return (update, new_momentum)


def solution(mesh):
    in_specs = (P("dp", "tensor", None), P("dp", "tensor", None), P())
    out_specs = (P(None, "tensor", None), P("dp", "tensor", None))
    return jax.shard_map(
        per_device, mesh=mesh, in_specs=in_specs, out_specs=out_specs, check_vma=False
    )
```

profile of v0, /device:TPU:0, one launch (start us, length us, event | category | flops | bytes accessed | tf_op | source)
XLA Modules:
  0.0 286.8 jit_solution(11792428714496908145)
XLA Ops:
  7.2 0.0 copy-start.1
  7.2 0.0 all-gather.2.cloned.1.call-start
  7.2 2.9 %multiply_reduce_fusion = (f32[]{:T(128)}, f32[1,72,6144]{2,1,0:T(8,128)S(1)}) fusion(bf16[1,72,6144]{2,1,0:T(8,128)(2,1)} %param.3, f32[1,72,6144]{2,1,0:T(8,128)} %param.4), kind=kLoop, calls=%fused_computation.8 | loop fusion | flops 3096575 | bytes 4423684 | tf_op jit(solution)/shard_map/reduce_sum | solution.py:20
  10.1 0.0 copy-start
  10.1 23.8 %psum.21 = f32[]{:T(128)} all-reduce(f32[]{:T(128)} %get-tuple-element.8), channel_id=1, replica_groups=mesh['dp'=4,'tensor'=8] {'tensor'}, use_global_device_ids=true, to_apply=%region_1.0 | all-reduce | flops 1 | bytes 8 | tf_op jit(solution)/shard_map/psum | solution.py:20
  34.6 0.0 copy-done.1
  34.6 0.3 divide_convert_fusion
  34.8 0.0 copy-done
  34.9 0.2 copy.16
  35.0 0.2 copy.12
  35.2 21.7 %all_to_all.29 = bf16[72,8,768]{2,0,1:T(8,128)(2,1)S(1)} all-to-all(bf16[72,8,768]{2,0,1:T(8,128)(2,1)S(1)} %copy.12), channel_id=1, replica_groups=mesh['dp'=4,'tensor'=8] {'tensor'}, dimensions={1} | all-to-all | bytes 1769472 | tf_op jit(solution)/shard_map/all_to_all | solution.py:22
  56.9 0.9 fusion.17
  57.7 79.9 %all-reduce.2 = bf16[576,576]{1,0:T(8,128)(2,1)S(1)} all-reduce(f32[576,576]{1,0:T(8,128)S(1)} %fusion.17), channel_id=1, replica_groups=mesh['dp'=4,'tensor'=8] {'tensor'}, use_global_device_ids=true, to_apply=%region_2.0 | all-reduce | flops 331776 | bytes 1990656 | tf_op jit(solution)/shard_map/psum | solution.py:24
  137.6 1.6 add_convert_fusion.1
  139.3 0.0 copy-start.3
  139.3 0.9 copy-done.3
  140.2 0.9 fusion.18
  141.1 0.0 copy-start.4
  141.1 78.1 %all-reduce.3 = bf16[576,576]{1,0:T(8,128)(2,1)S(1)} all-reduce(f32[576,576]{1,0:T(8,128)S(1)} %fusion.18), channel_id=1, replica_groups=mesh['dp'=4,'tensor'=8] {'tensor'}, use_global_device_ids=true, to_apply=%region_3.0 | all-reduce | flops 331776 | bytes 1990656 | tf_op jit(solution)/shard_map/psum | solution.py:24
  219.2 0.0 copy-done.4
  219.2 1.6 add_convert_fusion
  220.8 18.7 %all_to_all.30 = bf16[8,72,768]{2,1,0:T(8,128)(2,1)S(1)} all-to-all(bf16[8,72,768]{2,1,0:T(8,128)(2,1)S(1)} %bitcast.26), channel_id=1, replica_groups=mesh['dp'=4,'tensor'=8] {'tensor'}, dimensions={0} | all-to-all | bytes 1769472 | tf_op jit(solution)/shard_map/all_to_all | solution.py:32
  239.6 0.2 fusion.1
  239.7 0.2 copy.13
  239.9 0.0 copy-start.2
  239.9 1.3 convert_element_type.89
  241.2 0.0 all-gather.2.cloned.1.call-update
  241.2 28.5 %all-gather.2.cloned.1.call-done = bf16[4,72,6144]{2,1,0:T(8,128)(2,1)} async-done(((bf16[1,72,6144]{2,1,0:T(8,128)(2,1)}), bf16[4,72,6144]{2,1,0:T(8,128)(2,1)}) %all-gather.2.cloned.1.call-update) | async-done | bytes 3538960 | tf_op jit(solution)/shard_map/all_gather | solution.py:34
  269.7 0.0 copy-done.2
  269.7 6.5 %convolution_convert_fusion = bf16[4,72,6144]{2,0,1:T(4,128)(2,1)S(1)} fusion(bf16[4,72,6144]{2,1,0:T(8,128)(2,1)} %all-gather.2.cloned.1.call-done, s32[4]{0:T(128)S(1)} %copy-done.2), kind=kOutput, calls=%fused_computation | convolution fusion | flops 15925264 | bytes 7077904 | tf_op jit(solution)/shard_map/mg,grn->mrn/dot_general | solution.py:37
  276.2 3.7 %copy.15 = bf16[4,72,6144]{2,1,0:T(8,128)(2,1)} copy(bf16[4,72,6144]{2,0,1:T(4,128)(2,1)S(1)} %convolution_convert_fusion) | data formatting | bytes 7077888
Async XLA Ops:
  7.2 27.4 %copy-start.1 = (bf16[1,72,6144]{2,1,0:T(8,128)(2,1)S(1)}, bf16[1,72,6144]{2,1,0:T(8,128)(2,1)}, u32[]{:S(2)}) copy-start(bf16[1,72,6144]{2,1,0:T(8,128)(2,1)} %param.3) | copy-start | bytes 2654212
  7.2 262.5 %all-gather.2.cloned.1.call-start = ((), (), s32[]{:S(2)}) async-start(), calls=%async_computation.2 | async-start | bytes 4423680 | tf_op jit(solution)/shard_map/all_gather | solution.py:34
  10.1 24.7 %copy-start = (f32[1,72,6144]{2,1,0:T(8,128)}, f32[1,72,6144]{2,1,0:T(8,128)S(1)}, u32[]{:S(2)}) copy-start(f32[1,72,6144]{2,1,0:T(8,128)S(1)} %get-tuple-element.9) | copy-start | bytes 5308420
  139.3 0.9 copy-start.3
  141.1 78.1 %copy-start.4 = (bf16[576,768]{1,0:T(8,128)(2,1)S(1)}, bf16[576,768]{1,0:T(8,128)(2,1)}, u32[]{:S(2)}) copy-start(bf16[576,768]{1,0:T(8,128)(2,1)} %copy-done.3) | copy-start | bytes 2654212
  239.9 29.8 %copy-start.2 = (s32[4]{0:T(128)S(1)}, s32[4]{0:T(128)}, u32[]{:S(2)}) copy-start(s32[4]{0:T(128)} %param.5) | copy-start | bytes 52
Sparse Core Ops, SparseCore 0:
  241.3 28.2 all-gather.1
where the time goes:
time: 287 us
  blocking collectives  222 us (77%)
  waiting for transfers between devices  28.5 us (10%)
  between operations  14.8 us (5%)
  matrix products  11.6 us (4%)
  local copies, waits for them, and re-layouts  6.44 us (2%)
  other arithmetic  3.29 us (1%)
    psum x2, blocking collectives, per_device(): lax.psum(jnp.dot(columns, columns.T, preferred_element_type=jnp.float32),...  158 us
    all_gather x1, waiting for transfers between devices, per_device(): every_slot = lax.all_gather(scaled[None], 'dp', axis=0, tiled=True)  28.5 us
    psum x1, blocking collectives, per_device(): total = lax.psum(jnp.sum(direction * direction), 'tensor')  23.8 us
    all_to_all x1, blocking collectives, per_device(): lax.all_to_all(rows_here, 'tensor', split_axis=1, concat_axis=0, tiled=True)  21.7 us
    all_to_all x1, blocking collectives, per_device(): lax.all_to_all(columns, 'tensor', split_axis=0, concat_axis=1, tiled=True)  18.7 us
    dot_general x1, matrix products, per_device(): jnp.einsum('mg,grn->mrn', selector, every_slot, preferred_element_type=jn...  6.52 us
  transfers between devices with their start and end apart: 1, of which 1 were waited for; matrix products, arithmetic and copies ran while one was open for 0% of the time, Pallas kernels for 0%

commit v1 on v0

--- a/solution.py
+++ b/solution.py
@@ -21,8 +21,11 @@
     rows_here = (direction[0] / (jnp.sqrt(total) + eps)).astype(jnp.bfloat16)
     columns = lax.all_to_all(rows_here, "tensor", split_axis=1, concat_axis=0, tiled=True)
     for step in range(ITERS):
-        gram = lax.psum(
-            jnp.dot(columns, columns.T, preferred_element_type=jnp.float32), "tensor"
+        gram = jnp.sum(
+            lax.all_gather(
+                jnp.dot(columns, columns.T, preferred_element_type=jnp.float32), "tensor"
+            ),
+            axis=0,
         ).astype(jnp.bfloat16)
         square = jnp.dot(gram, gram, preferred_element_type=jnp.float32)
         poly = (coef_b * gram.astype(jnp.float32) + coef_c * square).astype(jnp.bfloat16)

time: 287 us -> 479 us (1.67)
  waiting for transfers between devices: 28.5 us -> 359 us
  blocking collectives: 222 us -> 70.7 us
  other arithmetic: 3.29 us -> 14.1 us
    all_gather x0 -> x2, waiting for transfers between devices: none -> 330 us  [per_device(): lax.all_gather(jnp.dot(columns, columns.T, preferred_element_type=jnp.flo...]
    psum x2 -> x0, blocking collectives: 158 us -> none  [per_device(): lax.psum(jnp.dot(columns, columns.T, preferred_element_type=jnp.float32),...]
    reduce_sum x0 -> x2, other arithmetic: none -> 10.8 us  [per_device(): jnp.sum(lax.all_gather(jnp.dot(columns, columns.T, preferred_element_type...]
    all_to_all x1, blocking collectives: 18.7 us -> 25.3 us  [per_device(): lax.all_to_all(columns, 'tensor', split_axis=0, concat_axis=1, tiled=True)]
  transfers between devices with their start and end apart: 1 -> 3, of which waited for: 1 -> 3; matrix products, arithmetic and copies ran while one was open for 0% -> 0% of each run, Pallas kernels for 0% -> 0%
where the time goes in v1:
time: 479 us; the launch traced here: 478 us
  waiting for transfers between devices  359 us (75%)
  blocking collectives  70.7 us (15%)
  between operations  14.5 us (3%)
  other arithmetic  14.1 us (3%)
  matrix products  13.8 us (3%)
  local copies, waits for them, and re-layouts  5.53 us (1%)
    all_gather x2, waiting for transfers between devices, per_device(): lax.all_gather(jnp.dot(columns, columns.T, preferred_element_type=jnp.flo...  330 us
    all_gather x1, waiting for transfers between devices, per_device(): every_slot = lax.all_gather(scaled[None], 'dp', axis=0, tiled=True)  29.4 us
    all_to_all x1, blocking collectives, per_device(): lax.all_to_all(columns, 'tensor', split_axis=0, concat_axis=1, tiled=True)  25.3 us
    psum x1, blocking collectives, per_device(): total = lax.psum(jnp.sum(direction * direction), 'tensor')  23.8 us
    all_to_all x1, blocking collectives, per_device(): lax.all_to_all(rows_here, 'tensor', split_axis=1, concat_axis=0, tiled=True)  21.7 us
    reduce_sum x2, other arithmetic, per_device(): jnp.sum(lax.all_gather(jnp.dot(columns, columns.T, preferred_element_type...  10.8 us
  transfers between devices with their start and end apart: 3, of which 3 were waited for; matrix products, arithmetic and copies ran while one was open for 0% of the time, Pallas kernels for 0%

profile of v1, /device:TPU:0, one launch (start us, length us, event | category | flops | bytes accessed | tf_op | source)
XLA Modules:
  0.0 478.2 jit_solution(2772929307619578020)
XLA Ops:
  7.2 0.0 copy-start.1
  7.2 0.0 all-gather.8.cloned.1.call-start
  7.2 2.9 multiply_reduce_fusion
  10.1 0.0 copy-start
  10.1 23.8 %psum.7 = f32[]{:T(128)} all-reduce(f32[]{:T(128)} %get-tuple-element.8), channel_id=1, replica_groups=mesh['dp'=4,'tensor'=8] {'tensor'}, use_global_device_ids=true, to_apply=%region_1.0 | all-reduce | flops 1 | bytes 8 | tf_op jit(solution)/shard_map/psum | solution.py:20
  34.6 0.0 copy-done.1
  34.6 0.3 divide_convert_fusion
  34.8 0.0 copy-done
  34.9 0.2 copy.16
  35.0 0.2 copy.12
  35.2 21.7 %all_to_all.29 = bf16[72,8,768]{2,0,1:T(8,128)(2,1)S(1)} all-to-all(bf16[72,8,768]{2,0,1:T(8,128)(2,1)S(1)} %copy.12), channel_id=1, replica_groups=mesh['dp'=4,'tensor'=8] {'tensor'}, dimensions={1} | all-to-all | bytes 1769472 | tf_op jit(solution)/shard_map/all_to_all | solution.py:22
  56.9 2.0 fusion.17
  58.9 0.0 all-gather.8.cloned.1.call-update
  58.9 0.0 all-gather.10.cloned.1.call-start
  58.9 165.1 %all-gather.8.cloned.1.call-done = f32[4608,576]{1,0:T(8,128)} async-done(((f32[576,576]{1,0:T(8,128)}), f32[4608,576]{1,0:T(8,128)}) %all-gather.8.cloned.1.call-update) | async-done | bytes 10616848 | tf_op jit(solution)/shard_map/all_gather | solution.py:25
  224.1 5.4 %reduce_sum.28 = bf16[576,576]{1,0:T(8,128)(2,1)S(1)} reduce(f32[8,576,576]{2,1,0:T(8,128)} %bitcast.25, f32[]{:T(128)} %constant.1.clone.1), dimensions={0}, to_apply=%region_2.0 | reduce | flops 2322432 | bytes 11280388 | tf_op jit(solution)/shard_map/reduce_sum | solution.py:24
  229.5 1.6 add_convert_fusion.1
  231.1 2.0 fusion.18
  233.1 0.0 all-gather.10.cloned.1.call-update
  233.2 0.0 all-gather.6.cloned.1.call-start
  233.2 164.8 %all-gather.10.cloned.1.call-done = f32[4608,576]{1,0:T(8,128)} async-done(((f32[576,576]{1,0:T(8,128)}), f32[4608,576]{1,0:T(8,128)}) %all-gather.10.cloned.1.call-update) | async-done | bytes 10616848 | tf_op jit(solution)/shard_map/all_gather | solution.py:25
  398.0 5.4 %reduce_sum.29 = bf16[576,576]{1,0:T(8,128)(2,1)S(1)} reduce(f32[8,576,576]{2,1,0:T(8,128)} %bitcast.24, f32[]{:T(128)} %constant.1.clone.1), dimensions={0}, to_apply=%region_3.0 | reduce | flops 2322432 | bytes 11280388 | tf_op jit(solution)/shard_map/reduce_sum | solution.py:24
  403.4 1.6 add_convert_fusion
  405.0 25.3 %all_to_all.30 = bf16[8,72,768]{2,1,0:T(8,128)(2,1)S(1)} all-to-all(bf16[8,72,768]{2,1,0:T(8,128)(2,1)S(1)} %bitcast.30), channel_id=1, replica_groups=mesh['dp'=4,'tensor'=8] {'tensor'}, dimensions={0} | all-to-all | bytes 1769472 | tf_op jit(solution)/shard_map/all_to_all | solution.py:35
  430.3 0.2 fusion.1
  430.5 0.2 copy.13
  430.6 0.0 copy-start.2
  430.7 1.3 convert_element_type.89
  432.0 0.0 all-gather.6.cloned.1.call-update
  432.0 29.4 %all-gather.6.cloned.1.call-done = bf16[4,72,6144]{2,1,0:T(8,128)(2,1)} async-done(((bf16[1,72,6144]{2,1,0:T(8,128)(2,1)}), bf16[4,72,6144]{2,1,0:T(8,128)(2,1)}) %all-gather.6.cloned.1.call-update) | async-done | bytes 3538960 | tf_op jit(solution)/shard_map/all_gather | solution.py:37
  461.4 0.0 copy-done.2
  461.4 6.5 %convolution_convert_fusion = bf16[4,72,6144]{2,0,1:T(4,128)(2,1)S(1)} fusion(bf16[4,72,6144]{2,1,0:T(8,128)(2,1)} %all-gather.6.cloned.1.call-done, s32[4]{0:T(128)S(1)} %copy-done.2), kind=kOutput, calls=%fused_computation | convolution fusion | flops 15925264 | bytes 7077904 | tf_op jit(solution)/shard_map/mg,grn->mrn/dot_general | solution.py:40
  467.9 3.7 copy.15
Async XLA Ops:
  7.2 27.4 %copy-start.1 = (bf16[1,72,6144]{2,1,0:T(8,128)(2,1)S(1)}, bf16[1,72,6144]{2,1,0:T(8,128)(2,1)}, u32[]{:S(2)}) copy-start(bf16[1,72,6144]{2,1,0:T(8,128)(2,1)} %param.3) | copy-start | bytes 2654212
  7.2 216.9 %all-gather.8.cloned.1.call-start = ((), (), s32[]{:S(2)}) async-start(), calls=%async_computation.3 | async-start | bytes 13271040 | tf_op jit(solution)/shard_map/all_gather | solution.py:25
  10.1 24.7 %copy-start = (f32[1,72,6144]{2,1,0:T(8,128)}, f32[1,72,6144]{2,1,0:T(8,128)S(1)}, u32[]{:S(2)}) copy-start(f32[1,72,6144]{2,1,0:T(8,128)S(1)} %get-tuple-element.9) | copy-start | bytes 5308420
  58.9 339.1 %all-gather.10.cloned.1.call-start = ((), (), s32[]{:S(2)}) async-start(), calls=%async_computation.4 | async-start | bytes 13271040 | tf_op jit(solution)/shard_map/all_gather | solution.py:25
  233.2 228.2 %all-gather.6.cloned.1.call-start = ((), (), s32[]{:S(2)}) async-start(), calls=%async_computation.2 | async-start | bytes 4423680 | tf_op jit(solution)/shard_map/all_gather | solution.py:37
  430.6 30.8 %copy-start.2 = (s32[4]{0:T(128)S(1)}, s32[4]{0:T(128)}, u32[]{:S(2)}) copy-start(s32[4]{0:T(128)} %param.5) | copy-start | bytes 52
Sparse Core Ops, SparseCore 0:
  59.0 165.0 all-gather.7
  233.3 164.6 all-gather.9
  432.1 29.2 all-gather.5
